TPU v7x, 128 devices: a whole 4x4x4 slice. The times are simulated.
128 devices in a mesh: gx: 16 (over z, x), gy: 8 (over y, core).
Axes of the slice: x: 4, y: 4, z: 4, core: 2. Of those that a mesh axis runs over, the one named last changes fastest.
Arguments:
- parent_field: float32 [8, 2048, 4096], P(None, 'gx', 'gy'), may hold values from -6 to 6
- parent_sppt: bfloat16 [2048, 4096], P('gx', 'gy'), may hold values from -0.796875 to 0.796875
- child_storm: float32 [8, 2048, 3072], P(None, 'gx', 'gy'), may hold values from -6 to 6
- child_sppt: bfloat16 [2048, 3072], P('gx', 'gy'), may hold values from -0.796875 to 0.796875
- wind: float32 [2, 8], replicated, may hold values from -0.3 to 0.3
- strip_dest: int32 [16384, 1], replicated, may hold values from 0 to 127; in each aligned block of 128 rows (0 to 127, 128 to 255, ...) at most 2 rows name the same one
- strip_row: int32 [16384], replicated, may hold values from 0 to 511
- strip_target: int32 [16384], replicated, may hold values from 0 to 127
- storm_shift: int32 [2, 4], replicated, may hold values from 0 to 15, as said below
Outputs:
- new_parent: float32 [8, 2048, 4096], P(None, 'gx', 'gy')
- child: float32 [8, 2048, 3072], P(None, 'gx', 'gy')
Inputs may be any that keep to these rules, and one draw needn't show every extreme that they name: `strip_dest`: among the 128 strips of one parent device no owner appears more than 2 times. `storm_shift`: row 0 lies in 0 to 16 - 1 and holds 16 - 1 at least once; row 1 lies in 0 to 8 - 1 and holds 8 - 1 at least once.
All inputs are finite; a program needn't handle non-finite values.
Results may differ from a plain program's by a relative error of at most 0.0003.
Values sent between devices are 32-bit elements; how exact they have to be, the bound alone decides.
No kernel may reach another device: no remote copies, remote signals or barrier semaphores. Data moves between devices by JAX's collectives and lax.ppermute only.
A program may use at most 64 MiB of HBM per device.

v0:
```python
import jax
import jax.numpy as jnp
from jax import lax
from jax.sharding import PartitionSpec as P

SUBSTEPS = 3
STRIP = 128
CAP = 2
KAPPA = 0.1
VERTICAL = 0.1
NUDGE = 0.5


def edge_halos(block):

    def swap(edge, axis, forward):
        count = lax.axis_size(axis)
        pairs = [(i, i + 1) for i in range(count - 1)]
        if not forward:
            pairs = [(target, source) for source, target in pairs]
        return lax.ppermute(edge, axis, pairs)

    before_x = swap(block[:, -1, :], "gx", True)
    after_x = swap(block[:, 0, :], "gx", False)
    before_y = swap(block[:, :, -1], "gy", True)
    after_y = swap(block[:, :, 0], "gy", False)
    return (before_x, after_x, before_y, after_y)


def halo_tendency(block, wind_x, wind_y):
    before_x, after_x, before_y, after_y = edge_halos(block)
    north = jnp.concatenate([block[:, 1:, :], after_x[:, None, :]], axis=1)
    south = jnp.concatenate([before_x[:, None, :], block[:, :-1, :]], axis=1)
    east = jnp.concatenate([block[:, :, 1:], after_y[:, :, None]], axis=2)
    west = jnp.concatenate([before_y[:, :, None], block[:, :, :-1]], axis=2)
    laplace = north + south + east + west - 4.0 * block
    return KAPPA * laplace - wind_x * (0.5 * (north - south)) - wind_y * (0.5 * (east - west))


def from_behind(value, axis, steps):
    count = lax.axis_size(axis)
    pairs = [(source, (source + steps) % count) for source in range(count)]
    return lax.ppermute(value, axis, pairs)


def storm_rows(child, storm_shift, nx, ny):
    levels, crows, widths = child.shape
    mine = lax.axis_index(("gx", "gy"))
    gathered = lax.all_to_all(child, ("gx", "gy"), 1, 1, tiled=True)
    piece = mine // (crows // storm_shift.shape[1])
    grid = gathered.reshape(levels, nx, ny, widths)
    grid = jnp.roll(grid, storm_shift[0, piece], axis=1)
    grid = jnp.roll(grid, storm_shift[1, piece], axis=2)
    return lax.all_to_all(grid.reshape(levels, crows, widths), ("gx", "gy"), 1, 1, tiled=True)


def refine_table(strip):
    coarse = jnp.arange(strip).astype(jnp.float32)
    finer = jnp.arange(3 * strip).astype(jnp.float32)
    position = jnp.clip((finer + 0.5) / 3.0 - 0.5, 0.0, strip - 1.0)
    return jnp.maximum(0.0, 1.0 - jnp.abs(position[None, :] - coarse[:, None]))


def vertical(field):
    upper = jnp.concatenate([field[1:], field[-1:]], axis=0)
    lower = jnp.concatenate([field[:1], field[:-1]], axis=0)
    return upper + lower - 2.0 * field


def shards(
    parent_field,
    parent_sppt,
    child_storm,
    child_sppt,
    wind,
    strip_dest,
    strip_row,
    strip_target,
    storm_shift,
):
    devices = lax.axis_size(("gx", "gy"))
    my_index = lax.axis_index(("gx", "gy"))
    wind_x = wind[0][:, None, None]
    wind_y = wind[1][:, None, None]
    new_parent = parent_field + (1.0 + parent_sppt.astype(jnp.float32)) * (
        halo_tendency(parent_field, wind_x, wind_y) + VERTICAL * vertical(parent_field)
    )
    levels, crows, widths = child_storm.shape
    npiece = storm_shift.shape[1]
    band_rows = crows // npiece
    nx, ny = (lax.axis_size("gx"), lax.axis_size("gy"))
    child = storm_rows(child_storm, storm_shift, nx, ny)
    dest_table = strip_dest.reshape(devices, -1)
    row_table = strip_row.reshape(devices, -1)
    target_table = strip_target.reshape(devices, -1)
    slots = dest_table.shape[1]
    my_dest = lax.dynamic_index_in_dim(dest_table, my_index, 0, keepdims=False)
    my_rows = lax.dynamic_index_in_dim(row_table, my_index, 0, keepdims=False)
    same_owner = my_dest[:, None] == my_dest[None, :]
    earlier = jnp.arange(slots)[None, :] < jnp.arange(slots)[:, None]
    rank = jnp.sum((same_owner & earlier).astype(jnp.int32), axis=1)
    slot_index = my_dest * CAP + rank
    send_select = (jnp.arange(devices * CAP)[:, None] == slot_index[None, :]).astype(jnp.float32)
    both_states = jnp.stack([parent_field, new_parent]).reshape(2, levels, -1, STRIP)
    picked = jnp.take(both_states, my_rows, axis=2)
    strip_values = jnp.moveaxis(picked, 2, 0).reshape(slots, -1)
    outgoing_strips = jnp.dot(
        send_select,
        strip_values,
        precision=lax.Precision.HIGHEST,
        preferred_element_type=jnp.float32,
    )
    incoming = lax.all_to_all(
        outgoing_strips, ("gx", "gy"), split_axis=0, concat_axis=0, tiled=True
    )
    mine = dest_table == my_index
    rank_all = jnp.cumsum(mine.astype(jnp.int32), axis=1) - 1
    slot_ids = jnp.arange(CAP)
    hits = mine[:, None, :] & (rank_all[:, None, :] == slot_ids[None, :, None])
    chosen = jnp.sum(jnp.where(hits, target_table[:, None, :], 0), axis=2)
    target_rows = jnp.where(jnp.any(hits, axis=2), chosen, -1).reshape(-1)
    row_select = (jnp.arange(crows)[:, None] == target_rows[None, :]).astype(jnp.float32)
    coarse = jnp.dot(
        row_select, incoming, precision=lax.Precision.HIGHEST, preferred_element_type=jnp.float32
    )
    counts = jnp.sum(row_select, axis=1)
    boundary = jnp.einsum(
        "tald,de->alte",
        coarse.reshape(crows, 2, levels, STRIP),
        refine_table(STRIP),
        precision=lax.Precision.HIGHEST,
    )
    divisor = 1.0 + NUDGE * counts[None, :, None]
    factor = 1.0 + child_sppt.astype(jnp.float32)
    for substep in range(SUBSTEPS):
        weight = (substep + 1) / 3.0
        target_value = boundary[0] + weight * (boundary[1] - boundary[0])
        child = (
            child + factor * halo_tendency(child, wind_x, wind_y) + NUDGE * target_value
        ) / divisor
    return (new_parent, child)


def solution(mesh):
    placed = (
        P(None, "gx", "gy"),
        P("gx", "gy"),
        P(None, "gx", "gy"),
        P("gx", "gy"),
        P(),
        P(),
        P(),
        P(),
        P(),
    )
    return jax.shard_map(
        shards,
        mesh=mesh,
        in_specs=placed,
        out_specs=(P(None, "gx", "gy"), P(None, "gx", "gy")),
        check_vma=False,
    )
```

profile of v0, /device:TPU:40, one launch (start us, length us, event | category | flops | bytes accessed | tf_op | source)
XLA Modules:
  0.0 225.1 jit_solution(2498742965248244502)
XLA Ops:
  2.4 1.9 collective-permute-start.3
  4.5 3.6 %collective-permute-start.2 = (f32[8,128]{1,0:T(8,128)S(1)}, f32[8,128]{1,0:T(8,128)S(1)}, u32[]{:S(2)}, u32[]{:S(2)}) collective-permute-start(f32[8,128]{1,0:T(8,128)S(1)} %bitcast.132), channel_id=1, source_target_pairs={{1,0},{2,1},{3,2},{4,3},{5,4},{6,5},{7,6},{9,8},{10,9},{11,10},{12... | collective-permute-start | bytes 12296 | tf_op jit(solution)/shard_map/ppermute | solution.py:21
  8.2 3.4 %collective-permute-start.1 = (f32[8,512]{1,0:T(8,128)S(1)}, f32[8,512]{1,0:T(8,128)S(1)}, u32[]{:S(2)}, u32[]{:S(2)}) collective-permute-start(f32[8,512]{1,0:T(8,128)S(1)} %bitcast.120), channel_id=1, source_target_pairs={{0,8},{8,16},{16,24},{24,32},{32,40},{40,48},{48,56},{56,64},{64,7... | collective-permute-start | bytes 49160 | tf_op jit(solution)/shard_map/ppermute | solution.py:21
  11.6 4.6 %collective-permute-start = (f32[8,512]{1,0:T(8,128)S(1)}, f32[8,512]{1,0:T(8,128)S(1)}, u32[]{:S(2)}, u32[]{:S(2)}) collective-permute-start(f32[8,512]{1,0:T(8,128)S(1)} %bitcast.122), channel_id=1, source_target_pairs={{8,0},{16,8},{24,16},{32,24},{40,32},{48,40},{56,48},{64,56},{72,6... | collective-permute-start | bytes 49160 | tf_op jit(solution)/shard_map/ppermute | solution.py:21
  16.2 3.5 %copy.138 = f32[8,128,384]{2,0,1:T(8,128)} copy(f32[8,128,384]{2,1,0:T(8,128)} %param.11) | data formatting | bytes 3145728 | tf_op args[2]
  19.7 8.5 %all-to-all-start = ((f32[8,128,384]{2,0,1:T(8,128)}), f32[8,128,384]{2,0,1:T(8,128)}, u32[]{:S(2)}, u32[]{:S(2)}) async-start(f32[8,128,384]{2,0,1:T(8,128)} %copy.138), calls=%async_computation | async-start | bytes 3145728 | tf_op jit(solution)/shard_map/all_to_all | solution.py:49
  29.0 2.5 %fusion.40 = (f32[7,128,512]{2,1,0:T(8,128)}, f32[7,128,512]{2,1,0:T(8,128)}) fusion(f32[8,128,512]{2,1,0:T(8,128)S(1)} %copy-done), kind=kLoop, calls=%fused_computation.104 | loop fusion | bytes 7340032 | tf_op jit(solution)/shard_map/slice | solution.py:66
  31.5 2.8 %fusion.37 = (f32[8,128,511]{2,1,0:T(8,128)}, f32[8,128,511]{2,1,0:T(8,128)}) fusion(f32[8,128,512]{2,1,0:T(8,128)S(1)} %copy-done), kind=kLoop, calls=%fused_computation.101 | loop fusion | bytes 8372224 | tf_op jit(solution)/shard_map/slice | solution.py:34
  34.2 2.5 %fusion.35 = (f32[8,127,512]{2,1,0:T(8,128)}, f32[8,127,512]{2,1,0:T(8,128)}) fusion(f32[8,128,512]{2,1,0:T(8,128)S(1)} %copy-done), kind=kLoop, calls=%fused_computation.99 | loop fusion | bytes 8323072 | tf_op jit(solution)/shard_map/slice | solution.py:32
  41.3 4.2 %copy.155 = f32[1,8,512,128]{3,1,2,0:T(8,128)} copy(f32[1,8,512,128]{3,2,1,0:T(8,128)} %stack.9) | data formatting | bytes 4194304 | tf_op jit(solution)/shard_map/stack | solution.py:104
  47.3 7.0 %fusion.4 = f32[8,128,512]{2,1,0:T(8,128)} fusion(f32[8,128,512]{2,1,0:T(8,128)S(1)} %copy-done, f32[1,128,512]{2,1,0:T(8,128)} %get-tuple-element.27, f32[7,128,512]{2,1,0:T(8,128)} %get-tuple-element.29, f32[7,128,512]{2,1,0:T(8,128)} %get-tuple-element.28, f32[1,128,512]{2,1,0:T(8,128)} %get-tuple-element.26, f32[8,128,511]{2,1,0:T(8,128)} %get-tuple-element.23, ...), kind=kLoop, calls=%fused_computation.15 | loop fusion | flops 13107200 | bytes 17039424 | tf_op jit(solution)/shard_map/add | solution.py:85
  57.6 2.2 pad_maximum_fusion
  59.8 2.9 %gather_fusion = f32[128,2,8,128]{3,2,1,0:T(8,128)S(1)} fusion(f32[2,8,512,128]{3,1,2,0:T(8,128)} %pad_maximum_fusion, s32[1024]{0:T(1024)S(1)} %pad_clamp_fusion), kind=kCustom, calls=%fused_computation | custom fusion | bytes 2097664 | tf_op jit(solution)/shard_map/jit(_take)/gather | solution.py:105
  64.6 3.0 %copy.157 = f32[128,2,2048]{2,1,0:T(2,128)} copy(f32[128,2,2048]{2,0,1:T(8,128)S(1)} %fusion.19) | data formatting | bytes 4194304 | tf_op jit(solution)/shard_map/dot_general | solution.py:107
  67.5 9.8 %all-to-all-start.2 = ((f32[128,2,2048]{2,1,0:T(2,128)}), f32[128,2,2048]{2,1,0:T(2,128)S(1)}, u32[]{:S(2)}, u32[]{:S(2)}) async-start(f32[128,2,2048]{2,1,0:T(2,128)} %copy.157), calls=%async_computation.2 | async-start | bytes 4194304 | tf_op jit(solution)/shard_map/all_to_all | solution.py:113
  82.3 1.7 copy.185
  84.7 2.1 copy.140
  86.8 17.8 %all-to-all-done.2 = f32[128,2,2048]{2,1,0:T(2,128)S(1)} async-done(((f32[128,2,2048]{2,1,0:T(2,128)}), f32[128,2,2048]{2,1,0:T(2,128)S(1)}, u32[]{:S(2)}, u32[]{:S(2)}) %all-to-all-start.2) | async-done | bytes 2097184 | tf_op jit(solution)/shard_map/all_to_all | solution.py:113
  105.9 7.7 %all-to-all-start.1 = ((f32[8,128,384]{2,0,1:T(8,128)}), f32[8,128,384]{2,0,1:T(8,128)S(1)}, u32[]{:S(2)}, u32[]{:S(2)}) async-start(f32[8,128,384]{2,0,1:T(8,128)} %copy.140), calls=%async_computation.1 | async-start | bytes 3145728 | tf_op jit(solution)/shard_map/all_to_all | solution.py:54
  114.2 3.6 %all_to_all.15 = f32[256,2048]{1,0:T(8,128)} reshape(f32[128,2,2048]{2,1,0:T(2,128)} %copy-done.1) | data formatting | bytes 4194304 | tf_op jit(solution)/shard_map/all_to_all | solution.py:113
  117.8 2.9 %copy.158 = f32[2048,256]{1,0:T(8,128)} copy(f32[2048,256]{0,1:T(8,128)} %bitcast.114) | data formatting | bytes 4194304 | tf_op jit(solution)/shard_map/dot_general | solution.py:123
  120.7 2.9 %fusion.15 = f32[128,2,8,128]{3,0,2,1:T(8,128)S(1)} fusion(f32[2,8,128,256]{3,2,1,0:T(8,128)} %bitcast.113, s32[256]{0:T(256)S(1)} %select_n.83), kind=kOutput, calls=%fused_computation.56 | convolution fusion | flops 805339136 | bytes 3146752 | tf_op jit(solution)/shard_map/dot_general | solution.py:123
  123.5 4.4 %convolution_bitcast_fusion = f32[2,8,128,384]{2,3,1,0:T(8,128)} fusion(f32[128,2,8,128]{3,0,2,1:T(8,128)S(1)} %fusion.15, f32[128]{0:T(128)S(1)} %iota_convert_fusion, f32[384]{0:T(512)S(1)} %add_clamp_fusion), kind=kOutput, calls=%fused_computation.16 | convolution fusion | flops 1208156160 | bytes 4196352 | tf_op jit(solution)/shard_map/tald,de->alte/dot_general | solution.py:127
  127.9 7.3 %all-to-all-done.1 = f32[8,128,384]{2,0,1:T(8,128)S(1)} async-done(((f32[8,128,384]{2,0,1:T(8,128)}), f32[8,128,384]{2,0,1:T(8,128)S(1)}, u32[]{:S(2)}, u32[]{:S(2)}) %all-to-all-start.1) | async-done | bytes 1572896 | tf_op jit(solution)/shard_map/all_to_all | solution.py:54
  135.8 1.9 fusion.48
  140.1 1.9 collective-permute-start.7
  143.3 3.9 %collective-permute-start.6 = (f32[8,128]{1,0:T(8,128)S(1)}, f32[8,128]{1,0:T(8,128)S(1)}, u32[]{:S(2)}, u32[]{:S(2)}) collective-permute-start(f32[8,128]{1,0:T(8,128)S(1)} %bitcast.141), channel_id=1, source_target_pairs={{1,0},{2,1},{3,2},{4,3},{5,4},{6,5},{7,6},{9,8},{10,9},{11,10},{12... | collective-permute-start | bytes 12296 | tf_op jit(solution)/shard_map/ppermute | solution.py:21
  147.1 2.7 %collective-permute-start.5 = (f32[8,384]{1,0:T(8,128)S(1)}, f32[8,384]{1,0:T(8,128)S(1)}, u32[]{:S(2)}, u32[]{:S(2)}) collective-permute-start(f32[8,384]{1,0:T(8,128)S(1)} %get-tuple-element.45), channel_id=1, source_target_pairs={{0,8},{8,16},{16,24},{24,32},{32,40},{40,48},{48,56},{56,64},{64,7... | collective-permute-start | bytes 36872 | tf_op jit(solution)/shard_map/ppermute | solution.py:21
  149.9 5.4 %collective-permute-start.4 = (f32[8,384]{1,0:T(8,128)S(1)}, f32[8,384]{1,0:T(8,128)S(1)}, u32[]{:S(2)}, u32[]{:S(2)}) collective-permute-start(f32[8,384]{1,0:T(8,128)S(1)} %get-tuple-element.44), channel_id=1, source_target_pairs={{8,0},{16,8},{24,16},{32,24},{40,32},{48,40},{56,48},{64,56},{72,6... | collective-permute-start | bytes 36872 | tf_op jit(solution)/shard_map/ppermute | solution.py:21
  155.3 2.2 fusion.47
  157.5 1.8 copy.145
  160.9 5.5 %add_divide_fusion.2 = f32[8,128,384]{1,2,0:T(8,128)S(1)} fusion(f32[8,128,384]{1,2,0:T(8,128)S(1)} %copy.151, f32[8,128,383]{1,2,0:T(8,128)} %get-tuple-element.47, f32[8,128,1]{1,2,0:T(1,128)S(1)} %bitcast.134, f32[8,128,1]{1,2,0:T(1,128)S(1)} %bitcast.137, f32[8,128,383]{1,2,0:T(8,128)} %get-tuple-element.46, f32[8,127,384]{1,2,0:T(8,128)} %get-tuple-element.43, ...), kind=kLoop, calls=%fused_computation.42 | loop fusion | flops 9437184 | bytes 12780096 | tf_op jit(solution)/shard_map/div | solution.py:138
  166.4 1.9 fusion.45
  169.7 1.9 collective-permute-start.11
  171.6 3.6 %collective-permute-start.10 = (f32[8,128]{1,0:T(8,128)S(1)}, f32[8,128]{1,0:T(8,128)S(1)}, u32[]{:S(2)}, u32[]{:S(2)}) collective-permute-start(f32[8,128]{1,0:T(8,128)S(1)} %bitcast.142), channel_id=1, source_target_pairs={{1,0},{2,1},{3,2},{4,3},{5,4},{6,5},{7,6},{9,8},{10,9},{11,10},{12... | collective-permute-start | bytes 12296 | tf_op jit(solution)/shard_map/ppermute | solution.py:21
  175.2 1.9 collective-permute-start.9
  177.2 6.0 %collective-permute-start.8 = (f32[8,384]{1,0:T(8,128)S(1)}, f32[8,384]{1,0:T(8,128)S(1)}, u32[]{:S(2)}, u32[]{:S(2)}) collective-permute-start(f32[8,384]{1,0:T(8,128)S(1)} %get-tuple-element.14), channel_id=1, source_target_pairs={{8,0},{16,8},{24,16},{32,24},{40,32},{48,40},{56,48},{64,56},{72,6... | collective-permute-start | bytes 36872 | tf_op jit(solution)/shard_map/ppermute | solution.py:21
  183.2 2.2 fusion.44
  185.4 1.8 copy.161
  188.8 5.5 %add_divide_fusion.1 = f32[8,128,384]{1,2,0:T(8,128)S(1)} fusion(f32[8,128,384]{1,2,0:T(8,128)S(1)} %add_divide_fusion.2, f32[8,128,383]{1,2,0:T(8,128)} %get-tuple-element.39, f32[8,128,1]{1,2,0:T(1,128)S(1)} %bitcast.138, f32[8,128,1]{1,2,0:T(1,128)S(1)} %bitcast.140, f32[8,128,383]{1,2,0:T(8,128)} %get-tuple-element.38, ...), kind=kLoop, calls=%fused_computation.41 | loop fusion | flops 9437184 | bytes 12780096 | tf_op jit(solution)/shard_map/div | solution.py:138
  197.0 1.9 collective-permute-start.15
  198.9 3.6 %collective-permute-start.14 = (f32[8,128]{1,0:T(8,128)S(1)}, f32[8,128]{1,0:T(8,128)S(1)}, u32[]{:S(2)}, u32[]{:S(2)}) collective-permute-start(f32[8,128]{1,0:T(8,128)S(1)} %bitcast.143), channel_id=1, source_target_pairs={{1,0},{2,1},{3,2},{4,3},{5,4},{6,5},{7,6},{9,8},{10,9},{11,10},{12... | collective-permute-start | bytes 12296 | tf_op jit(solution)/shard_map/ppermute | solution.py:21
  202.6 1.9 collective-permute-start.13
  204.5 6.0 %collective-permute-start.12 = (f32[8,384]{1,0:T(8,128)S(1)}, f32[8,384]{1,0:T(8,128)S(1)}, u32[]{:S(2)}, u32[]{:S(2)}) collective-permute-start(f32[8,384]{1,0:T(8,128)S(1)} %get-tuple-element.12), channel_id=1, source_target_pairs={{8,0},{16,8},{24,16},{32,24},{40,32},{48,40},{56,48},{64,56},{72,6... | collective-permute-start | bytes 36872 | tf_op jit(solution)/shard_map/ppermute | solution.py:21
  210.6 2.2 fusion.41
  214.4 1.8 copy.164
  216.2 5.9 %add_divide_fusion = f32[8,128,384]{1,2,0:T(8,128)} fusion(f32[8,128,384]{1,2,0:T(8,128)S(1)} %add_divide_fusion.1, f32[8,128,383]{1,2,0:T(8,128)} %get-tuple-element.33, f32[8,128,1]{1,2,0:T(1,128)S(1)} %bitcast.135, f32[8,128,1]{1,2,0:T(1,128)S(1)} %bitcast.136, f32[8,128,383]{1,2,0:T(8,128)S(1)} %get-tuple-element.32, ...), kind=kLoop, calls=%fused_computation.40 | loop fusion | flops 9043968 | bytes 12780096 | tf_op jit(solution)/shard_map/div | solution.py:138
  222.1 3.0 %copy.168 = f32[8,128,384]{2,1,0:T(8,128)} copy(f32[8,128,384]{1,2,0:T(8,128)} %add_divide_fusion) | data formatting | bytes 3145728
  (101 shorter events, 31.1 us)
Async XLA Ops:
  0.6 7.5 %copy-start = (f32[8,128,512]{2,1,0:T(8,128)S(1)}, f32[8,128,512]{2,1,0:T(8,128)}, u32[]{:S(2)}) copy-start(f32[8,128,512]{2,1,0:T(8,128)} %param.9) | copy-start | bytes 6291460
  2.4 43.1 %collective-permute-start.3 = (f32[8,128]{1,0:T(8,128)S(1)}, f32[8,128]{1,0:T(8,128)S(1)}, u32[]{:S(2)}, u32[]{:S(2)}) collective-permute-start(f32[8,128]{1,0:T(8,128)S(1)} %bitcast.130), channel_id=1, source_target_pairs={{0,1},{1,2},{2,3},{3,4},{4,5},{5,6},{6,7},{8,9},{9,10},{10,11},{11... | collective-permute-start | bytes 12296 | tf_op jit(solution)/shard_map/ppermute | solution.py:21
  4.5 41.3 %collective-permute-start.2 = (f32[8,128]{1,0:T(8,128)S(1)}, f32[8,128]{1,0:T(8,128)S(1)}, u32[]{:S(2)}, u32[]{:S(2)}) collective-permute-start(f32[8,128]{1,0:T(8,128)S(1)} %bitcast.132), channel_id=1, source_target_pairs={{1,0},{2,1},{3,2},{4,3},{5,4},{6,5},{7,6},{9,8},{10,9},{11,10},{12... | collective-permute-start | bytes 12296 | tf_op jit(solution)/shard_map/ppermute | solution.py:21
  8.2 39.1 %collective-permute-start.1 = (f32[8,512]{1,0:T(8,128)S(1)}, f32[8,512]{1,0:T(8,128)S(1)}, u32[]{:S(2)}, u32[]{:S(2)}) collective-permute-start(f32[8,512]{1,0:T(8,128)S(1)} %bitcast.120), channel_id=1, source_target_pairs={{0,8},{8,16},{16,24},{24,32},{32,40},{40,48},{48,56},{56,64},{64,7... | collective-permute-start | bytes 49160 | tf_op jit(solution)/shard_map/ppermute | solution.py:21
  11.6 35.7 %collective-permute-start = (f32[8,512]{1,0:T(8,128)S(1)}, f32[8,512]{1,0:T(8,128)S(1)}, u32[]{:S(2)}, u32[]{:S(2)}) collective-permute-start(f32[8,512]{1,0:T(8,128)S(1)} %bitcast.122), channel_id=1, source_target_pairs={{8,0},{16,8},{24,16},{32,24},{40,32},{48,40},{56,48},{64,56},{72,6... | collective-permute-start | bytes 49160 | tf_op jit(solution)/shard_map/ppermute | solution.py:21
  19.7 47.9 %all-to-all-start = ((f32[8,128,384]{2,0,1:T(8,128)}), f32[8,128,384]{2,0,1:T(8,128)}, u32[]{:S(2)}, u32[]{:S(2)}) async-start(f32[8,128,384]{2,0,1:T(8,128)} %copy.138), calls=%async_computation | async-start | bytes 3145728 | tf_op jit(solution)/shard_map/all_to_all | solution.py:49
  34.2 2.5 %copy-start.10 = (f32[2,8]{1,0:T(2,128)S(1)}, f32[2,8]{1,0:T(2,128)}, u32[]{:S(2)}) copy-start(f32[2,8]{1,0:T(2,128)} %param.13) | copy-start | bytes 196
  34.2 2.5 %copy-start.3 = (bf16[128,512]{1,0:T(8,128)(2,1)S(1)}, bf16[128,512]{1,0:T(8,128)(2,1)}, u32[]{:S(2)}) copy-start(bf16[128,512]{1,0:T(8,128)(2,1)} %param.10) | copy-start | bytes 393220
  34.2 3.3 %copy-start.5 = (s32[16384,1]{0,1:T(1,128)S(1)}, s32[16384,1]{0,1:T(1,128)}, u32[]{:S(2)}) copy-start(s32[16384,1]{0,1:T(1,128)} %param.14) | copy-start | bytes 196612
  45.8 0.6 copy-start.7
  56.0 1.6 copy-start.2
  59.8 2.9 %copy-start.12 = (pred[128]{0:T(512)(128)(4,1)S(1)}, pred[128]{0:T(512)(128)(4,1)}, u32[]{:S(2)}) copy-start(pred[128]{0:T(512)(128)(4,1)} %compare_and_fusion) | copy-start | bytes 388
  62.9 0.6 copy-start.8
  62.9 0.6 copy-start.9
  67.5 9.8 %copy-start.11 = (s32[2,4]{1,0:T(2,128)S(1)}, s32[2,4]{1,0:T(2,128)}, u32[]{:S(2)}) copy-start(s32[2,4]{1,0:T(2,128)} %param.17) | copy-start | bytes 100
  67.5 14.6 %copy-start.6 = (s32[16384]{0:T(1024)S(1)}, s32[16384]{0:T(1024)}, u32[]{:S(2)}) copy-start(s32[16384]{0:T(1024)} %param.16) | copy-start | bytes 196612
  67.5 37.1 %all-to-all-start.2 = ((f32[128,2,2048]{2,1,0:T(2,128)}), f32[128,2,2048]{2,1,0:T(2,128)S(1)}, u32[]{:S(2)}, u32[]{:S(2)}) async-start(f32[128,2,2048]{2,1,0:T(2,128)} %copy.157), calls=%async_computation.2 | async-start | bytes 4194304 | tf_op jit(solution)/shard_map/all_to_all | solution.py:113
  86.8 27.1 %copy-start.4 = (bf16[128,384]{1,0:T(8,128)(2,1)S(1)}, bf16[128,384]{1,0:T(8,128)(2,1)}, u32[]{:S(2)}) copy-start(bf16[128,384]{1,0:T(8,128)(2,1)} %param.12) | copy-start | bytes 294916
  104.6 1.3 copy-start.1
  105.9 29.3 %all-to-all-start.1 = ((f32[8,128,384]{2,0,1:T(8,128)}), f32[8,128,384]{2,0,1:T(8,128)S(1)}, u32[]{:S(2)}, u32[]{:S(2)}) async-start(f32[8,128,384]{2,0,1:T(8,128)} %copy.140), calls=%async_computation.1 | async-start | bytes 3145728 | tf_op jit(solution)/shard_map/all_to_all | solution.py:54
  140.1 20.8 %collective-permute-start.7 = (f32[8,128]{1,0:T(8,128)S(1)}, f32[8,128]{1,0:T(8,128)S(1)}, u32[]{:S(2)}, u32[]{:S(2)}) collective-permute-start(f32[8,128]{1,0:T(8,128)S(1)} %bitcast.139), channel_id=1, source_target_pairs={{0,1},{1,2},{2,3},{3,4},{4,5},{5,6},{6,7},{8,9},{9,10},{10,11},{11... | collective-permute-start | bytes 12296 | tf_op jit(solution)/shard_map/ppermute | solution.py:21
  143.3 17.7 %collective-permute-start.6 = (f32[8,128]{1,0:T(8,128)S(1)}, f32[8,128]{1,0:T(8,128)S(1)}, u32[]{:S(2)}, u32[]{:S(2)}) collective-permute-start(f32[8,128]{1,0:T(8,128)S(1)} %bitcast.141), channel_id=1, source_target_pairs={{1,0},{2,1},{3,2},{4,3},{5,4},{6,5},{7,6},{9,8},{10,9},{11,10},{12... | collective-permute-start | bytes 12296 | tf_op jit(solution)/shard_map/ppermute | solution.py:21
  147.1 10.4 %collective-permute-start.5 = (f32[8,384]{1,0:T(8,128)S(1)}, f32[8,384]{1,0:T(8,128)S(1)}, u32[]{:S(2)}, u32[]{:S(2)}) collective-permute-start(f32[8,384]{1,0:T(8,128)S(1)} %get-tuple-element.45), channel_id=1, source_target_pairs={{0,8},{8,16},{16,24},{24,32},{32,40},{40,48},{48,56},{56,64},{64,7... | collective-permute-start | bytes 36872 | tf_op jit(solution)/shard_map/ppermute | solution.py:21
  149.9 9.4 %collective-permute-start.4 = (f32[8,384]{1,0:T(8,128)S(1)}, f32[8,384]{1,0:T(8,128)S(1)}, u32[]{:S(2)}, u32[]{:S(2)}) collective-permute-start(f32[8,384]{1,0:T(8,128)S(1)} %get-tuple-element.44), channel_id=1, source_target_pairs={{8,0},{16,8},{24,16},{32,24},{40,32},{48,40},{56,48},{64,56},{72,6... | collective-permute-start | bytes 36872 | tf_op jit(solution)/shard_map/ppermute | solution.py:21
  169.7 19.1 %collective-permute-start.11 = (f32[8,128]{1,0:T(8,128)S(1)}, f32[8,128]{1,0:T(8,128)S(1)}, u32[]{:S(2)}, u32[]{:S(2)}) collective-permute-start(f32[8,128]{1,0:T(8,128)S(1)} %bitcast.144), channel_id=1, source_target_pairs={{0,1},{1,2},{2,3},{3,4},{4,5},{5,6},{6,7},{8,9},{9,10},{10,11},{11... | collective-permute-start | bytes 12296 | tf_op jit(solution)/shard_map/ppermute | solution.py:21
  171.6 17.2 %collective-permute-start.10 = (f32[8,128]{1,0:T(8,128)S(1)}, f32[8,128]{1,0:T(8,128)S(1)}, u32[]{:S(2)}, u32[]{:S(2)}) collective-permute-start(f32[8,128]{1,0:T(8,128)S(1)} %bitcast.142), channel_id=1, source_target_pairs={{1,0},{2,1},{3,2},{4,3},{5,4},{6,5},{7,6},{9,8},{10,9},{11,10},{12... | collective-permute-start | bytes 12296 | tf_op jit(solution)/shard_map/ppermute | solution.py:21
  175.2 10.1 %collective-permute-start.9 = (f32[8,384]{1,0:T(8,128)S(1)}, f32[8,384]{1,0:T(8,128)S(1)}, u32[]{:S(2)}, u32[]{:S(2)}) collective-permute-start(f32[8,384]{1,0:T(8,128)S(1)} %get-tuple-element.15), channel_id=1, source_target_pairs={{0,8},{8,16},{16,24},{24,32},{32,40},{40,48},{48,56},{56,64},{64,7... | collective-permute-start | bytes 36872 | tf_op jit(solution)/shard_map/ppermute | solution.py:21
  177.2 10.0 %collective-permute-start.8 = (f32[8,384]{1,0:T(8,128)S(1)}, f32[8,384]{1,0:T(8,128)S(1)}, u32[]{:S(2)}, u32[]{:S(2)}) collective-permute-start(f32[8,384]{1,0:T(8,128)S(1)} %get-tuple-element.14), channel_id=1, source_target_pairs={{8,0},{16,8},{24,16},{32,24},{40,32},{48,40},{56,48},{64,56},{72,6... | collective-permute-start | bytes 36872 | tf_op jit(solution)/shard_map/ppermute | solution.py:21
  197.0 19.2 %collective-permute-start.15 = (f32[8,128]{1,0:T(8,128)S(1)}, f32[8,128]{1,0:T(8,128)S(1)}, u32[]{:S(2)}, u32[]{:S(2)}) collective-permute-start(f32[8,128]{1,0:T(8,128)S(1)} %bitcast.145), channel_id=1, source_target_pairs={{0,1},{1,2},{2,3},{3,4},{4,5},{5,6},{6,7},{8,9},{9,10},{10,11},{11... | collective-permute-start | bytes 12296 | tf_op jit(solution)/shard_map/ppermute | solution.py:21
  198.9 17.3 %collective-permute-start.14 = (f32[8,128]{1,0:T(8,128)S(1)}, f32[8,128]{1,0:T(8,128)S(1)}, u32[]{:S(2)}, u32[]{:S(2)}) collective-permute-start(f32[8,128]{1,0:T(8,128)S(1)} %bitcast.143), channel_id=1, source_target_pairs={{1,0},{2,1},{3,2},{4,3},{5,4},{6,5},{7,6},{9,8},{10,9},{11,10},{12... | collective-permute-start | bytes 12296 | tf_op jit(solution)/shard_map/ppermute | solution.py:21
  202.6 10.2 %collective-permute-start.13 = (f32[8,384]{1,0:T(8,128)S(1)}, f32[8,384]{1,0:T(8,128)S(1)}, u32[]{:S(2)}, u32[]{:S(2)}) collective-permute-start(f32[8,384]{1,0:T(8,128)S(1)} %get-tuple-element.13), channel_id=1, source_target_pairs={{0,8},{8,16},{16,24},{24,32},{32,40},{40,48},{48,56},{56,64},{64,7... | collective-permute-start | bytes 36872 | tf_op jit(solution)/shard_map/ppermute | solution.py:21
  204.5 9.9 %collective-permute-start.12 = (f32[8,384]{1,0:T(8,128)S(1)}, f32[8,384]{1,0:T(8,128)S(1)}, u32[]{:S(2)}, u32[]{:S(2)}) collective-permute-start(f32[8,384]{1,0:T(8,128)S(1)} %get-tuple-element.12), channel_id=1, source_target_pairs={{8,0},{16,8},{24,16},{32,24},{40,32},{48,40},{56,48},{64,56},{72,6... | collective-permute-start | bytes 36872 | tf_op jit(solution)/shard_map/ppermute | solution.py:21
where the time goes:
time: 226 us; the launch traced here: 225 us
  starting transfers between devices  80.4 us (36%)
  local copies, waits for them, and re-layouts  75.5 us (33%)
  other arithmetic  30.8 us (14%)
  waiting for transfers between devices  25.2 us (11%)
  matrix products  8.25 us (4%)
  between operations  4.92 us (2%)
    ppermute x16, starting transfers between devices, swap(): return lax.ppermute(edge, axis, pairs)  54.5 us
    all_to_all x1, waiting for transfers between devices, shards(): lax.all_to_all(outgoing_strips, ('gx', 'gy'), split_axis=0, concat_axis=0...  17.8 us
    div x3, other arithmetic, shards(): (child + factor * halo_tendency(child, wind_x, wind_y) + NUDGE * target_v...  16.9 us
    unnamed x34, local copies, waits for them, and re-layouts  12 us
    all_to_all x1, starting transfers between devices, shards(): lax.all_to_all(outgoing_strips, ('gx', 'gy'), split_axis=0, concat_axis=0...  9.77 us
    slice x4, local copies, waits for them, and re-layouts, halo_tendency(): north = jnp.concatenate([block[:, 1:, :], after_x[:, None, :]], axis=1)  9.01 us
    all_to_all x1, starting transfers between devices, storm_rows(): gathered = lax.all_to_all(child, ('gx', 'gy'), 1, 1, tiled=True)  8.47 us
    another operation x4, local copies, waits for them, and re-layouts, shards(): jnp.stack([parent_field, new_parent]).reshape(2, levels, -1, STRIP)  8.4 us
  transfers between devices with their start and end apart: 19, of which 2 were waited for; matrix products, arithmetic and copies ran while one was open for 34% of the time, Pallas kernels for 0%

commit v1 on v0

--- a/solution.py
+++ b/solution.py
@@ -2,6 +2,7 @@
 import jax.numpy as jnp
 from jax import lax
 from jax.sharding import PartitionSpec as P
+from jax.lax import all_to_all, axis_size
 
 SUBSTEPS = 3
 STRIP = 128
@@ -9,6 +10,14 @@
 KAPPA = 0.1
 VERTICAL = 0.1
 NUDGE = 0.5
+
+
+def seats_all_name(local_values, link_axis):
+    seen_now = axis_size(link_axis)
+    y1 = jnp.split(local_values, seen_now, 1)
+    mixed_arr = jnp.stack(y1, 0)
+    frame_out = all_to_all(mixed_arr, link_axis, 0, 0)
+    return jnp.concatenate(frame_out, 1)
 
 
 def edge_halos(block):
@@ -51,7 +60,7 @@
     grid = gathered.reshape(levels, nx, ny, widths)
     grid = jnp.roll(grid, storm_shift[0, piece], axis=1)
     grid = jnp.roll(grid, storm_shift[1, piece], axis=2)
-    return lax.all_to_all(grid.reshape(levels, crows, widths), ("gx", "gy"), 1, 1, tiled=True)
+    return seats_all_name(grid.reshape(levels, crows, widths), ("gx", "gy"))
 
 
 def refine_table(strip):

time: 226 us -> 282 us (1.25)
  local copies, waits for them, and re-layouts: 75.5 us -> 146 us
  waiting for transfers between devices: 25.2 us -> 10.8 us
    unnamed x34 -> x147, local copies, waits for them, and re-layouts: 12 us -> 83.1 us
    all_to_all x1, waiting for transfers between devices: 17.8 us -> 0.01 us  [shards(): lax.all_to_all(outgoing_strips, ('gx', 'gy'), split_axis=0, concat_axis=0...]
    all_to_all x1, waiting for transfers between devices: 7.35 us -> 10.7 us  [seats_all_name(): frame_out = all_to_all(mixed_arr, link_axis, 0, 0)]
  transfers between devices with their start and end apart: 19 -> 19, of which waited for: 2 -> 1; matrix products, arithmetic and copies ran while one was open for 34% -> 52% of each run, Pallas kernels for 0% -> 0%
where the time goes in v1:
time: 282 us; the launch traced here: 281 us
  local copies, waits for them, and re-layouts  146 us (52%)
  starting transfers between devices  82.9 us (29%)
  other arithmetic  29.3 us (10%)
  waiting for transfers between devices  10.8 us (4%)
  matrix products  6.67 us (2%)
  between operations  5.29 us (2%)
    unnamed x147, local copies, waits for them, and re-layouts  83.1 us
    ppermute x16, starting transfers between devices, swap(): return lax.ppermute(edge, axis, pairs)  54.5 us
    div x3, other arithmetic, shards(): (child + factor * halo_tendency(child, wind_x, wind_y) + NUDGE * target_v...  16.9 us
    all_to_all x1, waiting for transfers between devices, seats_all_name(): frame_out = all_to_all(mixed_arr, link_axis, 0, 0)  10.7 us
    all_to_all x1, starting transfers between devices, seats_all_name(): frame_out = all_to_all(mixed_arr, link_axis, 0, 0)  10.2 us
    all_to_all x1, starting transfers between devices, shards(): lax.all_to_all(outgoing_strips, ('gx', 'gy'), split_axis=0, concat_axis=0...  9.77 us
    slice x4, local copies, waits for them, and re-layouts, halo_tendency(): north = jnp.concatenate([block[:, 1:, :], after_x[:, None, :]], axis=1)  8.97 us
    all_to_all x1, starting transfers between devices, storm_rows(): gathered = lax.all_to_all(child, ('gx', 'gy'), 1, 1, tiled=True)  8.48 us
  transfers between devices with their start and end apart: 19, of which 1 were waited for; matrix products, arithmetic and copies ran while one was open for 52% of the time, Pallas kernels for 0%

profile of v1, /device:TPU:40, one launch (start us, length us, event | category | flops | bytes accessed | tf_op | source)
XLA Modules:
  0.0 280.9 jit_solution(1669845772374963624)
XLA Ops:
  0.6 1.7 slice_reduce_fusion.7
  2.3 1.9 collective-permute-start.3
  4.3 3.6 %collective-permute-start.2 = (f32[8,128]{1,0:T(8,128)S(1)}, f32[8,128]{1,0:T(8,128)S(1)}, u32[]{:S(2)}, u32[]{:S(2)}) collective-permute-start(f32[8,128]{1,0:T(8,128)S(1)} %get-tuple-element.70), channel_id=1, source_target_pairs={{1,0},{2,1},{3,2},{4,3},{5,4},{6,5},{7,6},{9,8},{10,9},{11,10},{12... | collective-permute-start | bytes 12296 | tf_op jit(solution)/shard_map/ppermute | solution.py:30
  8.9 3.4 %collective-permute-start.1 = (f32[8,512]{1,0:T(8,128)S(1)}, f32[8,512]{1,0:T(8,128)S(1)}, u32[]{:S(2)}, u32[]{:S(2)}) collective-permute-start(f32[8,512]{1,0:T(8,128)S(1)} %bitcast.752), channel_id=1, source_target_pairs={{0,8},{8,16},{16,24},{24,32},{32,40},{40,48},{48,56},{56,64},{64,7... | collective-permute-start | bytes 49160 | tf_op jit(solution)/shard_map/ppermute | solution.py:30
  12.3 4.6 %collective-permute-start = (f32[8,512]{1,0:T(8,128)S(1)}, f32[8,512]{1,0:T(8,128)S(1)}, u32[]{:S(2)}, u32[]{:S(2)}) collective-permute-start(f32[8,512]{1,0:T(8,128)S(1)} %bitcast.754), channel_id=1, source_target_pairs={{8,0},{16,8},{24,16},{32,24},{40,32},{48,40},{56,48},{64,56},{72,6... | collective-permute-start | bytes 49160 | tf_op jit(solution)/shard_map/ppermute | solution.py:30
  16.9 3.5 %copy.4947 = f32[8,128,384]{2,0,1:T(8,128)} copy(f32[8,128,384]{2,1,0:T(8,128)} %param.11) | data formatting | bytes 3145728 | tf_op args[2]
  20.4 8.5 %all-to-all-start = ((f32[8,128,384]{2,0,1:T(8,128)}), f32[8,128,384]{2,0,1:T(8,128)}, u32[]{:S(2)}, u32[]{:S(2)}) async-start(f32[8,128,384]{2,0,1:T(8,128)} %copy.4947), calls=%async_computation | async-start | bytes 3145728 | tf_op jit(solution)/shard_map/all_to_all | solution.py:58
  29.8 2.5 fusion.38
  32.2 2.8 fusion.36
  35.0 2.5 fusion.34
  45.9 4.2 %copy.4957 = f32[1,8,512,128]{3,1,2,0:T(8,128)} copy(f32[1,8,512,128]{3,2,1,0:T(8,128)} %stack.525) | data formatting | bytes 4194304 | tf_op jit(solution)/shard_map/stack | solution.py:113
  50.7 7.0 %fusion.4 = f32[8,128,512]{2,1,0:T(8,128)} fusion(f32[8,128,512]{2,1,0:T(8,128)S(1)} %copy-done, f32[1,128,512]{2,1,0:T(8,128)} %get-tuple-element.87, f32[7,128,512]{2,1,0:T(8,128)} %get-tuple-element.89, f32[7,128,512]{2,1,0:T(8,128)} %get-tuple-element.88, f32[1,128,512]{2,1,0:T(8,128)} %get-tuple-element.86, f32[8,128,511]{2,1,0:T(8,128)} %get-tuple-element.85, ...), kind=kLoop, calls=%fused_computation.15 | loop fusion | flops 13107200 | bytes 17039424 | tf_op jit(solution)/shard_map/add | solution.py:94
  60.9 2.2 pad_maximum_fusion
  63.1 2.9 %gather_fusion = f32[128,2,8,128]{3,2,1,0:T(8,128)S(1)} fusion(f32[2,8,512,128]{3,1,2,0:T(8,128)} %pad_maximum_fusion, s32[1024]{0:T(1024)S(1)} %pad_clamp_fusion), kind=kCustom, calls=%fused_computation | custom fusion | bytes 2097664 | tf_op jit(solution)/shard_map/jit(_take)/gather | solution.py:114
  67.4 2.9 %copy.4959 = f32[128,2,2048]{2,1,0:T(2,128)} copy(f32[128,2,2048]{2,0,1:T(8,128)S(1)} %fusion.18) | data formatting | bytes 4194304 | tf_op jit(solution)/shard_map/dot_general | solution.py:116
  70.4 9.8 %all-to-all-start.2 = ((f32[128,2,2048]{2,1,0:T(2,128)}), f32[128,2,2048]{2,1,0:T(2,128)S(1)}, u32[]{:S(2)}, u32[]{:S(2)}) async-start(f32[128,2,2048]{2,1,0:T(2,128)} %copy.4959), calls=%async_computation.2 | async-start | bytes 4194304 | tf_op jit(solution)/shard_map/all_to_all | solution.py:122
  80.1 1.7 copy.4975
  160.5 10.2 %all-to-all-start.1 = ((f32[128,8,1,384]{3,1,2,0:T(8,128)}), f32[128,8,1,384]{3,1,2,0:T(8,128)}, u32[]{:S(2)}, u32[]{:S(2)}) async-start(f32[128,8,1,384]{3,1,2,0:T(8,128)} %constant_dynamic-update-slice_fusion), calls=%async_computation.1 | async-start | bytes 3145728 | tf_op jit(solution)/shard_map/all_to_all | solution.py:19
  171.2 2.5 all_to_all.15
  173.7 1.9 copy.4960
  176.9 4.4 %convolution_bitcast_fusion = f32[2,8,128,384]{2,3,1,0:T(8,128)} fusion(f32[128,2,8,128]{3,0,2,1:T(8,128)S(1)} %fusion.14, f32[128]{0:T(128)S(1)} %iota_convert_fusion, f32[384]{0:T(512)S(1)} %add_clamp_fusion), kind=kOutput, calls=%fused_computation.16 | convolution fusion | flops 1208156160 | bytes 4196352 | tf_op jit(solution)/shard_map/tald,de->alte/dot_general | solution.py:136
  181.3 10.7 %all-to-all-done.1 = f32[128,8,1,384]{3,1,2,0:T(8,128)} async-done(((f32[128,8,1,384]{3,1,2,0:T(8,128)}), f32[128,8,1,384]{3,1,2,0:T(8,128)}, u32[]{:S(2)}, u32[]{:S(2)}) %all-to-all-start.1) | async-done | bytes 1572896 | tf_op jit(solution)/shard_map/all_to_all | solution.py:19
  192.0 1.9 copy.4950
  193.9 1.9 fusion.46
  197.1 1.9 collective-permute-start.7
  199.1 3.9 %collective-permute-start.6 = (f32[8,128]{1,0:T(8,128)S(1)}, f32[8,128]{1,0:T(8,128)S(1)}, u32[]{:S(2)}, u32[]{:S(2)}) collective-permute-start(f32[8,128]{1,0:T(8,128)S(1)} %bitcast.770), channel_id=1, source_target_pairs={{1,0},{2,1},{3,2},{4,3},{5,4},{6,5},{7,6},{9,8},{10,9},{11,10},{12... | collective-permute-start | bytes 12296 | tf_op jit(solution)/shard_map/ppermute | solution.py:30
  202.9 2.7 collective-permute-start.5
  205.7 5.5 %collective-permute-start.4 = (f32[8,384]{1,0:T(8,128)S(1)}, f32[8,384]{1,0:T(8,128)S(1)}, u32[]{:S(2)}, u32[]{:S(2)}) collective-permute-start(f32[8,384]{1,0:T(8,128)S(1)} %get-tuple-element.76), channel_id=1, source_target_pairs={{8,0},{16,8},{24,16},{32,24},{40,32},{48,40},{56,48},{64,56},{72,6... | collective-permute-start | bytes 36872 | tf_op jit(solution)/shard_map/ppermute | solution.py:30
  211.1 2.1 fusion.45
  213.3 1.8 copy.4953
  215.1 1.7 copy.4952
  216.7 5.5 %add_divide_fusion.2 = f32[8,128,384]{1,2,0:T(8,128)S(1)} fusion(f32[8,128,383]{1,2,0:T(8,128)} %get-tuple-element.105, f32[8,128,1]{1,2,0:T(1,128)S(1)} %bitcast.766, f32[8,128,1]{1,2,0:T(1,128)S(1)} %bitcast.768, f32[8,128,383]{1,2,0:T(8,128)} %get-tuple-element.104, f32[8,127,384]{1,2,0:T(8,128)} %get-tuple-element.103, f32[8,1,384]{1,2,0:T(8,128)} %copy.4953, ...), kind=kLoop, calls=%fused_computation.43 | loop fusion | flops 9437184 | bytes 12780096 | tf_op jit(solution)/shard_map/div | solution.py:147
  222.2 1.9 fusion.43
  225.5 1.9 collective-permute-start.11
  227.4 3.6 %collective-permute-start.10 = (f32[8,128]{1,0:T(8,128)S(1)}, f32[8,128]{1,0:T(8,128)S(1)}, u32[]{:S(2)}, u32[]{:S(2)}) collective-permute-start(f32[8,128]{1,0:T(8,128)S(1)} %bitcast.771), channel_id=1, source_target_pairs={{1,0},{2,1},{3,2},{4,3},{5,4},{6,5},{7,6},{9,8},{10,9},{11,10},{12... | collective-permute-start | bytes 12296 | tf_op jit(solution)/shard_map/ppermute | solution.py:30
  231.0 1.9 collective-permute-start.9
  233.0 6.0 %collective-permute-start.8 = (f32[8,384]{1,0:T(8,128)S(1)}, f32[8,384]{1,0:T(8,128)S(1)}, u32[]{:S(2)}, u32[]{:S(2)}) collective-permute-start(f32[8,384]{1,0:T(8,128)S(1)} %get-tuple-element.74), channel_id=1, source_target_pairs={{8,0},{16,8},{24,16},{32,24},{40,32},{48,40},{56,48},{64,56},{72,6... | collective-permute-start | bytes 36872 | tf_op jit(solution)/shard_map/ppermute | solution.py:30
  239.0 2.1 fusion.42
  241.2 1.8 copy.4963
  244.6 5.5 %add_divide_fusion.1 = f32[8,128,384]{1,2,0:T(8,128)S(1)} fusion(f32[8,128,384]{1,2,0:T(8,128)S(1)} %add_divide_fusion.2, f32[8,128,383]{1,2,0:T(8,128)} %get-tuple-element.99, f32[8,128,1]{1,2,0:T(1,128)S(1)} %bitcast.767, f32[8,128,1]{1,2,0:T(1,128)S(1)} %bitcast.769, f32[8,128,383]{1,2,0:T(8,128)} %get-tuple-element.98, ...), kind=kLoop, calls=%fused_computation.42 | loop fusion | flops 9437184 | bytes 12780096 | tf_op jit(solution)/shard_map/div | solution.py:147
  252.8 1.9 collective-permute-start.15
  254.7 3.6 %collective-permute-start.14 = (f32[8,128]{1,0:T(8,128)S(1)}, f32[8,128]{1,0:T(8,128)S(1)}, u32[]{:S(2)}, u32[]{:S(2)}) collective-permute-start(f32[8,128]{1,0:T(8,128)S(1)} %bitcast.772), channel_id=1, source_target_pairs={{1,0},{2,1},{3,2},{4,3},{5,4},{6,5},{7,6},{9,8},{10,9},{11,10},{12... | collective-permute-start | bytes 12296 | tf_op jit(solution)/shard_map/ppermute | solution.py:30
  258.4 1.9 collective-permute-start.13
  260.3 6.0 %collective-permute-start.12 = (f32[8,384]{1,0:T(8,128)S(1)}, f32[8,384]{1,0:T(8,128)S(1)}, u32[]{:S(2)}, u32[]{:S(2)}) collective-permute-start(f32[8,384]{1,0:T(8,128)S(1)} %get-tuple-element.72), channel_id=1, source_target_pairs={{8,0},{16,8},{24,16},{32,24},{40,32},{48,40},{56,48},{64,56},{72,6... | collective-permute-start | bytes 36872 | tf_op jit(solution)/shard_map/ppermute | solution.py:30
  266.4 2.2 fusion.39
  270.2 1.8 copy.4964
  272.0 5.9 %add_divide_fusion = f32[8,128,384]{1,2,0:T(8,128)} fusion(f32[8,128,384]{1,2,0:T(8,128)S(1)} %add_divide_fusion.1, f32[8,128,383]{1,2,0:T(8,128)} %get-tuple-element.93, f32[8,128,1]{1,2,0:T(1,128)S(1)} %bitcast.764, f32[8,128,1]{1,2,0:T(1,128)S(1)} %bitcast.765, f32[8,128,383]{1,2,0:T(8,128)S(1)} %get-tuple-element.92, ...), kind=kLoop, calls=%fused_computation.41 | loop fusion | flops 9043968 | bytes 12780096 | tf_op jit(solution)/shard_map/div | solution.py:147
  277.9 3.0 %copy.4966 = f32[8,128,384]{2,1,0:T(8,128)} copy(f32[8,128,384]{1,2,0:T(8,128)} %add_divide_fusion) | data formatting | bytes 3145728
  (215 shorter events, 100.3 us)
Async XLA Ops:
  2.3 47.8 %collective-permute-start.3 = (f32[8,128]{1,0:T(8,128)S(1)}, f32[8,128]{1,0:T(8,128)S(1)}, u32[]{:S(2)}, u32[]{:S(2)}) collective-permute-start(f32[8,128]{1,0:T(8,128)S(1)} %get-tuple-element.71), channel_id=1, source_target_pairs={{0,1},{1,2},{2,3},{3,4},{4,5},{5,6},{6,7},{8,9},{9,10},{10,11},{11... | collective-permute-start | bytes 12296 | tf_op jit(solution)/shard_map/ppermute | solution.py:30
  4.3 46.1 %collective-permute-start.2 = (f32[8,128]{1,0:T(8,128)S(1)}, f32[8,128]{1,0:T(8,128)S(1)}, u32[]{:S(2)}, u32[]{:S(2)}) collective-permute-start(f32[8,128]{1,0:T(8,128)S(1)} %get-tuple-element.70), channel_id=1, source_target_pairs={{1,0},{2,1},{3,2},{4,3},{5,4},{6,5},{7,6},{9,8},{10,9},{11,10},{12... | collective-permute-start | bytes 12296 | tf_op jit(solution)/shard_map/ppermute | solution.py:30
  8.9 41.7 %collective-permute-start.1 = (f32[8,512]{1,0:T(8,128)S(1)}, f32[8,512]{1,0:T(8,128)S(1)}, u32[]{:S(2)}, u32[]{:S(2)}) collective-permute-start(f32[8,512]{1,0:T(8,128)S(1)} %bitcast.752), channel_id=1, source_target_pairs={{0,8},{8,16},{16,24},{24,32},{32,40},{40,48},{48,56},{56,64},{64,7... | collective-permute-start | bytes 49160 | tf_op jit(solution)/shard_map/ppermute | solution.py:30
  12.3 38.3 %collective-permute-start = (f32[8,512]{1,0:T(8,128)S(1)}, f32[8,512]{1,0:T(8,128)S(1)}, u32[]{:S(2)}, u32[]{:S(2)}) collective-permute-start(f32[8,512]{1,0:T(8,128)S(1)} %bitcast.754), channel_id=1, source_target_pairs={{8,0},{16,8},{24,16},{32,24},{40,32},{48,40},{56,48},{64,56},{72,6... | collective-permute-start | bytes 49160 | tf_op jit(solution)/shard_map/ppermute | solution.py:30
  20.4 8.5 %copy-start = (f32[8,128,512]{2,1,0:T(8,128)S(1)}, f32[8,128,512]{2,1,0:T(8,128)}, u32[]{:S(2)}) copy-start(f32[8,128,512]{2,1,0:T(8,128)} %param.9) | copy-start | bytes 6291460
  20.4 50.0 %all-to-all-start = ((f32[8,128,384]{2,0,1:T(8,128)}), f32[8,128,384]{2,0,1:T(8,128)}, u32[]{:S(2)}, u32[]{:S(2)}) async-start(f32[8,128,384]{2,0,1:T(8,128)} %copy.4947), calls=%async_computation | async-start | bytes 3145728 | tf_op jit(solution)/shard_map/all_to_all | solution.py:58
  35.0 2.5 copy-start.6
  35.0 2.5 copy-start.2
  35.0 2.6 copy-start.4
  35.0 4.0 %copy-start.5 = (s32[16384]{0:T(1024)S(1)}, s32[16384]{0:T(1024)}, u32[]{:S(2)}) copy-start(s32[16384]{0:T(1024)} %param.16) | copy-start | bytes 196612
  35.0 4.8 %copy-start.7 = (s32[2,4]{1,0:T(2,128)S(1)}, s32[2,4]{1,0:T(2,128)}, u32[]{:S(2)}) copy-start(s32[2,4]{1,0:T(2,128)} %param.17) | copy-start | bytes 100
  59.3 1.6 copy-start.1
  70.4 90.1 %all-to-all-start.2 = ((f32[128,2,2048]{2,1,0:T(2,128)}), f32[128,2,2048]{2,1,0:T(2,128)S(1)}, u32[]{:S(2)}, u32[]{:S(2)}) async-start(f32[128,2,2048]{2,1,0:T(2,128)} %copy.4959), calls=%async_computation.2 | async-start | bytes 4194304 | tf_op jit(solution)/shard_map/all_to_all | solution.py:122
  160.5 10.4 %copy-start.3 = (bf16[128,384]{1,0:T(8,128)(2,1)S(1)}, bf16[128,384]{1,0:T(8,128)(2,1)}, u32[]{:S(2)}) copy-start(bf16[128,384]{1,0:T(8,128)(2,1)} %param.12) | copy-start | bytes 294916
  160.5 31.5 %all-to-all-start.1 = ((f32[128,8,1,384]{3,1,2,0:T(8,128)}), f32[128,8,1,384]{3,1,2,0:T(8,128)}, u32[]{:S(2)}, u32[]{:S(2)}) async-start(f32[128,8,1,384]{3,1,2,0:T(8,128)} %constant_dynamic-update-slice_fusion), calls=%async_computation.1 | async-start | bytes 3145728 | tf_op jit(solution)/shard_map/all_to_all | solution.py:19
  197.1 19.6 %collective-permute-start.7 = (f32[8,128]{1,0:T(8,128)S(1)}, f32[8,128]{1,0:T(8,128)S(1)}, u32[]{:S(2)}, u32[]{:S(2)}) collective-permute-start(f32[8,128]{1,0:T(8,128)S(1)} %bitcast.773), channel_id=1, source_target_pairs={{0,1},{1,2},{2,3},{3,4},{4,5},{5,6},{6,7},{8,9},{9,10},{10,11},{11... | collective-permute-start | bytes 12296 | tf_op jit(solution)/shard_map/ppermute | solution.py:30
  199.1 17.7 %collective-permute-start.6 = (f32[8,128]{1,0:T(8,128)S(1)}, f32[8,128]{1,0:T(8,128)S(1)}, u32[]{:S(2)}, u32[]{:S(2)}) collective-permute-start(f32[8,128]{1,0:T(8,128)S(1)} %bitcast.770), channel_id=1, source_target_pairs={{1,0},{2,1},{3,2},{4,3},{5,4},{6,5},{7,6},{9,8},{10,9},{11,10},{12... | collective-permute-start | bytes 12296 | tf_op jit(solution)/shard_map/ppermute | solution.py:30
  202.9 10.4 %collective-permute-start.5 = (f32[8,384]{1,0:T(8,128)S(1)}, f32[8,384]{1,0:T(8,128)S(1)}, u32[]{:S(2)}, u32[]{:S(2)}) collective-permute-start(f32[8,384]{1,0:T(8,128)S(1)} %get-tuple-element.77), channel_id=1, source_target_pairs={{0,8},{8,16},{16,24},{24,32},{32,40},{40,48},{48,56},{56,64},{64,7... | collective-permute-start | bytes 36872 | tf_op jit(solution)/shard_map/ppermute | solution.py:30
  205.7 9.4 %collective-permute-start.4 = (f32[8,384]{1,0:T(8,128)S(1)}, f32[8,384]{1,0:T(8,128)S(1)}, u32[]{:S(2)}, u32[]{:S(2)}) collective-permute-start(f32[8,384]{1,0:T(8,128)S(1)} %get-tuple-element.76), channel_id=1, source_target_pairs={{8,0},{16,8},{24,16},{32,24},{40,32},{48,40},{56,48},{64,56},{72,6... | collective-permute-start | bytes 36872 | tf_op jit(solution)/shard_map/ppermute | solution.py:30
  225.5 19.1 %collective-permute-start.11 = (f32[8,128]{1,0:T(8,128)S(1)}, f32[8,128]{1,0:T(8,128)S(1)}, u32[]{:S(2)}, u32[]{:S(2)}) collective-permute-start(f32[8,128]{1,0:T(8,128)S(1)} %bitcast.774), channel_id=1, source_target_pairs={{0,1},{1,2},{2,3},{3,4},{4,5},{5,6},{6,7},{8,9},{9,10},{10,11},{11... | collective-permute-start | bytes 12296 | tf_op jit(solution)/shard_map/ppermute | solution.py:30
  227.4 17.2 %collective-permute-start.10 = (f32[8,128]{1,0:T(8,128)S(1)}, f32[8,128]{1,0:T(8,128)S(1)}, u32[]{:S(2)}, u32[]{:S(2)}) collective-permute-start(f32[8,128]{1,0:T(8,128)S(1)} %bitcast.771), channel_id=1, source_target_pairs={{1,0},{2,1},{3,2},{4,3},{5,4},{6,5},{7,6},{9,8},{10,9},{11,10},{12... | collective-permute-start | bytes 12296 | tf_op jit(solution)/shard_map/ppermute | solution.py:30
  231.0 10.1 %collective-permute-start.9 = (f32[8,384]{1,0:T(8,128)S(1)}, f32[8,384]{1,0:T(8,128)S(1)}, u32[]{:S(2)}, u32[]{:S(2)}) collective-permute-start(f32[8,384]{1,0:T(8,128)S(1)} %get-tuple-element.75), channel_id=1, source_target_pairs={{0,8},{8,16},{16,24},{24,32},{32,40},{40,48},{48,56},{56,64},{64,7... | collective-permute-start | bytes 36872 | tf_op jit(solution)/shard_map/ppermute | solution.py:30
  233.0 9.9 %collective-permute-start.8 = (f32[8,384]{1,0:T(8,128)S(1)}, f32[8,384]{1,0:T(8,128)S(1)}, u32[]{:S(2)}, u32[]{:S(2)}) collective-permute-start(f32[8,384]{1,0:T(8,128)S(1)} %get-tuple-element.74), channel_id=1, source_target_pairs={{8,0},{16,8},{24,16},{32,24},{40,32},{48,40},{56,48},{64,56},{72,6... | collective-permute-start | bytes 36872 | tf_op jit(solution)/shard_map/ppermute | solution.py:30
  252.8 19.2 %collective-permute-start.15 = (f32[8,128]{1,0:T(8,128)S(1)}, f32[8,128]{1,0:T(8,128)S(1)}, u32[]{:S(2)}, u32[]{:S(2)}) collective-permute-start(f32[8,128]{1,0:T(8,128)S(1)} %bitcast.775), channel_id=1, source_target_pairs={{0,1},{1,2},{2,3},{3,4},{4,5},{5,6},{6,7},{8,9},{9,10},{10,11},{11... | collective-permute-start | bytes 12296 | tf_op jit(solution)/shard_map/ppermute | solution.py:30
  254.7 17.2 %collective-permute-start.14 = (f32[8,128]{1,0:T(8,128)S(1)}, f32[8,128]{1,0:T(8,128)S(1)}, u32[]{:S(2)}, u32[]{:S(2)}) collective-permute-start(f32[8,128]{1,0:T(8,128)S(1)} %bitcast.772), channel_id=1, source_target_pairs={{1,0},{2,1},{3,2},{4,3},{5,4},{6,5},{7,6},{9,8},{10,9},{11,10},{12... | collective-permute-start | bytes 12296 | tf_op jit(solution)/shard_map/ppermute | solution.py:30
  258.4 10.2 %collective-permute-start.13 = (f32[8,384]{1,0:T(8,128)S(1)}, f32[8,384]{1,0:T(8,128)S(1)}, u32[]{:S(2)}, u32[]{:S(2)}) collective-permute-start(f32[8,384]{1,0:T(8,128)S(1)} %get-tuple-element.73), channel_id=1, source_target_pairs={{0,8},{8,16},{16,24},{24,32},{32,40},{40,48},{48,56},{56,64},{64,7... | collective-permute-start | bytes 36872 | tf_op jit(solution)/shard_map/ppermute | solution.py:30
  260.3 9.9 %collective-permute-start.12 = (f32[8,384]{1,0:T(8,128)S(1)}, f32[8,384]{1,0:T(8,128)S(1)}, u32[]{:S(2)}, u32[]{:S(2)}) collective-permute-start(f32[8,384]{1,0:T(8,128)S(1)} %get-tuple-element.72), channel_id=1, source_target_pairs={{8,0},{16,8},{24,16},{32,24},{40,32},{48,40},{56,48},{64,56},{72,6... | collective-permute-start | bytes 36872 | tf_op jit(solution)/shard_map/ppermute | solution.py:30
